TPU v7x, 512 devices: a whole 4x4x16 slice. The times are simulated.
512 devices in a mesh: grp: 8 (over z_lo, core), spec: 64 (over z_hi, x, y).
Axes of the slice: x: 4, y: 4, z: 16 (z_hi: 4, z_lo: 4; z = z_hi * 4 + z_lo), core: 2. Of those that a mesh axis runs over, the one named last changes fastest.
Arguments:
- queries: bfloat16 [262144, 1024], P(('grp', 'spec')), may hold values from -6 to 6
- out_grad: bfloat16 [262144, 1024], P(('grp', 'spec')), may hold values from -48 to 48
- spec_keys: bfloat16 [512, 192, 1024], P(('grp', 'spec')), may hold values from -6 to 6
- spec_values: bfloat16 [512, 192, 1024], P(('grp', 'spec')), may hold values from -6 to 6
- owner_of: int32 [32768, 1], P(('grp', 'spec')), may hold values from 0 to 63; in each aligned block of 64 rows (0 to 63, 64 to 127, ...) at most 2 rows name the same one
- query_gain: float32 [1024], replicated, may hold values from 0.5 to 1.5
Outputs:
- query_grad: bfloat16 [262144, 1024], P(('grp', 'spec'))
- key_grad: bfloat16 [512, 192, 1024], P(('grp', 'spec'))
- value_grad: bfloat16 [512, 192, 1024], P(('grp', 'spec'))
- gain_grad: float32 [1024], replicated
Inputs may be any that keep to these rules, and one draw needn't show every extreme that they name: `owner_of`: among the candidates of one device, at most 2 name the same spec.
All inputs are finite; a program needn't handle non-finite values.
Results may differ from a plain program's by a relative error of at most 0.012.
The roundings to bfloat16 on the way count: a program that leaves them out, or rounds other values in their place, can miss the bound.
Values may be sent and summed in bfloat16 or wider, within the bound.
No kernel may reach another device: no remote copies, remote signals or barrier semaphores. Data moves between devices by JAX's collectives and lax.ppermute only.
A program may use at most 64 MiB of HBM per device.

v0:
```python
import math
import jax
import jax.numpy as jnp
from jax import lax
from jax.sharding import PartitionSpec as P

HEADS = 8
HEAD_DIM = 128
CAP = 2
PIECES = 2


def attend_backward(recv_rows, recv_grads, keys_here, values_here, query_gain):
    total_rows, _, head_dim = recv_rows.shape
    width = HEADS * head_dim
    key_count = keys_here.shape[0]
    inv_root = 1.0 / math.sqrt(HEAD_DIM)
    f32 = jnp.float32
    gain_hm = query_gain.reshape(HEADS, 1, head_dim)
    raw_hm = recv_rows.transpose(1, 0, 2)
    g_hm = recv_grads.transpose(1, 0, 2)
    k_hm = keys_here.reshape(key_count, HEADS, head_dim).transpose(1, 0, 2)
    v_hm = values_here.reshape(key_count, HEADS, head_dim).transpose(1, 0, 2)
    gained_hm = (raw_hm.astype(f32) * gain_hm).astype(jnp.bfloat16)
    scores = jnp.einsum("hrd,hkd->hrk", gained_hm, k_hm, preferred_element_type=f32) * inv_root
    top = jnp.max(scores, axis=2, keepdims=True)
    expo = jnp.exp(scores - top)
    probs = expo / jnp.sum(expo, axis=2, keepdims=True)
    probs_b = probs.astype(jnp.bfloat16)
    attended = jnp.einsum("hrk,hkd->hrd", probs_b, v_hm, preferred_element_type=f32)
    delta = jnp.sum(g_hm.astype(f32) * attended, axis=2, keepdims=True)
    dprobs = jnp.einsum("hrd,hkd->hrk", g_hm, v_hm, preferred_element_type=f32)
    dscores = (probs * (dprobs - delta)).astype(jnp.bfloat16)
    q_grad = jnp.einsum("hrk,hkd->hrd", dscores, k_hm, preferred_element_type=f32) * inv_root
    k_grad = jnp.einsum("hrk,hrd->hkd", dscores, gained_hm, preferred_element_type=f32) * inv_root
    v_grad = jnp.einsum("hrk,hrd->hkd", probs_b, g_hm, preferred_element_type=f32)
    gain_part = jnp.sum(raw_hm.astype(f32) * q_grad, axis=1).reshape(width)
    going_back = (q_grad * gain_hm).astype(jnp.bfloat16).transpose(1, 0, 2)
    key_grad = k_grad.astype(jnp.bfloat16).transpose(1, 0, 2).reshape(key_count, width)
    value_grad = v_grad.astype(jnp.bfloat16).transpose(1, 0, 2).reshape(key_count, width)
    return (going_back, gain_part, key_grad, value_grad)


def split_pieces(value, count):
    pieces = []
    rest = value
    for _ in range(count - 1):
        head = lax.reduce_precision(rest, exponent_bits=8, mantissa_bits=7)
        pieces.append(head)
        rest = rest - head
    pieces.append(rest)
    return jnp.stack(pieces).astype(jnp.bfloat16)


def shards(queries, out_grad, spec_keys, spec_values, owner_of, query_gain):
    peers = lax.axis_size("spec")
    cand_count = owner_of.shape[0]
    width = queries.shape[1]
    qtok_here = queries.shape[0] // cand_count
    slot_count = peers * CAP
    target = owner_of[:, 0]
    onehot = (target[:, None] == jnp.arange(peers, dtype=jnp.int32)[None, :]).astype(jnp.int32)
    earlier = jnp.cumsum(onehot, axis=0) - onehot
    position = jnp.sum(earlier * onehot, axis=1)
    slot_index = target * CAP + position
    matches = jnp.arange(slot_count, dtype=jnp.int32)[:, None] == slot_index[None, :]
    source = jnp.argmax(matches, axis=1).astype(jnp.int32)
    used = jnp.any(matches, axis=1)
    head_dim = width // HEADS
    both = jnp.concatenate(
        [
            queries.reshape(cand_count, qtok_here, HEADS, head_dim),
            out_grad.reshape(cand_count, qtok_here, HEADS, head_dim),
        ],
        axis=1,
    )
    both = jnp.pad(both, ((0, 1), (0, 0), (0, 0), (0, 0)))
    source = jnp.where(used, source, cand_count)
    send_both = jnp.take(both, source, axis=0, mode="clip")
    send_both = send_both.reshape(peers, CAP * 2 * qtok_here, HEADS, head_dim)
    recv_both = lax.all_to_all(send_both, "spec", split_axis=0, concat_axis=0, tiled=True)
    recv_both = recv_both.reshape(slot_count, 2, qtok_here, HEADS, head_dim)
    recv_rows = recv_both[:, 0].reshape(slot_count * qtok_here, HEADS, head_dim)
    recv_cotan = recv_both[:, 1].reshape(slot_count * qtok_here, HEADS, head_dim)
    going_back, partial_value, key_grad, value_grad = attend_backward(
        recv_rows, recv_cotan, spec_keys[0], spec_values[0], query_gain
    )
    going_back = going_back.reshape(peers, CAP * qtok_here, HEADS, width // HEADS)
    gain_rows = jnp.broadcast_to(
        split_pieces(partial_value, PIECES).reshape(1, PIECES, HEADS, width // HEADS),
        (peers, PIECES, HEADS, width // HEADS),
    )
    going_back = jnp.concatenate([going_back, gain_rows], axis=1)
    came_back = lax.all_to_all(going_back, "spec", split_axis=0, concat_axis=0, tiled=True)
    spec_sum = jnp.sum(came_back[:, CAP * qtok_here :].astype(jnp.float32), axis=(0, 1)).reshape(
        width
    )
    gain_grad = lax.psum(spec_sum, "grp")
    came_back = came_back[:, : CAP * qtok_here]
    home_grads = jnp.take(
        came_back.reshape(slot_count, qtok_here, HEADS, width // HEADS),
        slot_index,
        axis=0,
        mode="clip",
    )
    query_grad = home_grads.reshape(cand_count * qtok_here, width)
    return (query_grad, key_grad[None], value_grad[None], gain_grad)


def solution(mesh):
    return jax.shard_map(
        shards,
        mesh=mesh,
        in_specs=(
            P(("grp", "spec"), None),
            P(("grp", "spec"), None),
            P(("grp", "spec"), None, None),
            P(("grp", "spec"), None, None),
            P(("grp", "spec"), None),
            P(),
        ),
        out_specs=(
            P(("grp", "spec"), None),
            P(("grp", "spec"), None, None),
            P(("grp", "spec"), None, None),
            P(),
        ),
        check_vma=False,
    )
```

profile of v0, /device:TPU:1, one launch (start us, length us, event | category | flops | bytes accessed | tf_op | source)
XLA Modules:
  0.0 385.1 jit_solution(2665026931376670259)
XLA Ops:
  0.6 0.7 fusion.36
  1.4 0.1 reduce_window_sum.11
  1.5 0.8 select_reduce_fusion
  2.3 0.7 multiply_add_fusion
  3.0 0.6 iota_reduce_fusion
  3.6 0.1 fusion.37
  3.7 2.2 copy_bitcast_fusion.1
  5.9 0.2 fusion.10
  6.1 3.1 gather_fusion
  9.1 0.0 copy-start.3
  9.1 0.0 copy-start.4
  9.1 0.0 copy-start.6
  9.1 22.3 %all-to-all-start = ((bf16[64,32,8,128]{3,2,1,0:T(8,128)(2,1)}), bf16[64,32,8,128]{3,2,1,0:T(8,128)(2,1)}, u32[]{:S(2)}, u32[]{:S(2)}) async-start(bf16[64,32,8,128]{3,2,1,0:T(8,128)(2,1)} %bitcast.82), calls=%async_computation | async-start | bytes 8388608 | tf_op jit(solution)/shard_map/all_to_all | solution.py:81
  31.4 0.0 copy-done.3
  31.4 0.1 copy.46
  31.5 0.0 copy-done.4
  31.5 0.1 copy.47
  31.6 0.0 copy-done.6
  31.6 0.0 copy-start.5
  31.6 184.3 %all-to-all-done = bf16[64,32,8,128]{3,2,1,0:T(8,128)(2,1)} async-done(((bf16[64,32,8,128]{3,2,1,0:T(8,128)(2,1)}), bf16[64,32,8,128]{3,2,1,0:T(8,128)(2,1)}, u32[]{:S(2)}, u32[]{:S(2)}) %all-to-all-start) | async-done | bytes 4194336 | tf_op jit(solution)/shard_map/all_to_all | solution.py:81
  215.9 3.1 fusion.41
  219.0 0.0 copy-start.2
  219.0 0.0 copy-start
  219.0 1.4 fusion.25
  220.4 5.1 %fusion.42 = (f32[8,1024]{1,0:T(8,128)S(1)}, f32[8,1024,192]{1,2,0:T(8,128)S(1)}) fusion(f32[8,1024,192]{1,2,0:T(8,128)S(1)} %fusion.25), kind=kOutput, calls=%fused_computation.65 | output fusion | flops 6291647 | bytes 12615680 | tf_op jit(solution)/shard_map/sub | solution.py:27
  225.5 1.0 fusion.9
  226.5 0.0 copy-start.1
  226.5 0.0 copy-done.5
  226.5 2.3 multiply_reduce_fusion.1
  228.8 0.0 copy-done.2
  228.9 2.3 multiply_convert_fusion
  231.2 0.0 copy-done
  231.2 0.0 copy-done.1
  231.2 2.0 multiply_convert_fusion.1
  233.2 2.4 copy.40
  235.7 0.0 copy-start.7
  235.8 1.6 pad_maximum_fusion
  237.4 15.2 %all-to-all-start.1 = ((bf16[64,18,8,128]{3,2,1,0:T(8,128)(2,1)}), bf16[64,18,8,128]{3,2,1,0:T(8,128)(2,1)}, u32[]{:S(2)}, u32[]{:S(2)}) async-start(bf16[64,18,8,128]{3,2,1,0:T(8,128)(2,1)} %pad_maximum_fusion), calls=%async_computation.1 | async-start | bytes 4718592 | tf_op jit(solution)/shard_map/all_to_all | solution.py:94
  252.5 0.0 copy-done.7
  252.6 3.6 fusion.20
  256.2 0.3 copy.41
  256.5 0.9 broadcast_in_dim_reshape.6
  257.4 3.7 fusion.21
  261.1 0.3 copy.42
  261.4 0.9 broadcast_in_dim_reshape.7
  262.3 96.9 %all-to-all-done.1 = bf16[64,18,8,128]{3,2,1,0:T(8,128)(2,1)} async-done(((bf16[64,18,8,128]{3,2,1,0:T(8,128)(2,1)}), bf16[64,18,8,128]{3,2,1,0:T(8,128)(2,1)}, u32[]{:S(2)}, u32[]{:S(2)}) %all-to-all-start.1) | async-done | bytes 2359328 | tf_op jit(solution)/shard_map/all_to_all | solution.py:94
  359.2 1.7 slice.22
  360.9 0.7 gather_fusion.1
  361.7 1.2 copy.87
  362.9 1.1 convert_reduce_fusion
  364.0 21.0 %psum.7 = f32[1024]{0:T(1024)} all-reduce(f32[1024]{0:T(1024)S(1)} %bitcast.96), channel_id=1, replica_groups=mesh['grp'=8,'spec'=64] {'grp'}, use_global_device_ids=true, to_apply=%region_9.10 | all-reduce | flops 1024 | bytes 8192 | tf_op jit(solution)/shard_map/psum | solution.py:98
  (8 shorter events, 0.1 us)
Async XLA Ops:
  9.1 22.3 %copy-start.3 = (bf16[1,192,1024]{2,1,0:T(8,128)(2,1)S(1)}, bf16[1,192,1024]{2,1,0:T(8,128)(2,1)}, u32[]{:S(2)}) copy-start(bf16[1,192,1024]{2,1,0:T(8,128)(2,1)} %param.8) | copy-start | bytes 1179652
  9.1 22.4 %copy-start.4 = (bf16[1,192,1024]{2,1,0:T(8,128)(2,1)S(1)}, bf16[1,192,1024]{2,1,0:T(8,128)(2,1)}, u32[]{:S(2)}) copy-start(bf16[1,192,1024]{2,1,0:T(8,128)(2,1)} %param.9) | copy-start | bytes 1179652
  9.1 22.5 %copy-start.6 = (f32[1024]{0:T(1024)S(1)}, f32[1024]{0:T(1024)}, u32[]{:S(2)}) copy-start(f32[1024]{0:T(1024)} %param.11) | copy-start | bytes 12292
  9.1 206.8 %all-to-all-start = ((bf16[64,32,8,128]{3,2,1,0:T(8,128)(2,1)}), bf16[64,32,8,128]{3,2,1,0:T(8,128)(2,1)}, u32[]{:S(2)}, u32[]{:S(2)}) async-start(bf16[64,32,8,128]{3,2,1,0:T(8,128)(2,1)} %bitcast.82), calls=%async_computation | async-start | bytes 8388608 | tf_op jit(solution)/shard_map/all_to_all | solution.py:81
  31.6 194.9 %copy-start.5 = (bf16[24,8,8,128]{3,2,1,0:T(8,128)(2,1)}, bf16[24,8,8,128]{3,2,1,0:T(8,128)(2,1)S(1)}, u32[]{:S(2)}) copy-start(bf16[24,8,8,128]{3,2,1,0:T(8,128)(2,1)S(1)} %copy.47) | copy-start | bytes 1179652
  219.0 9.9 %copy-start.2 = (bf16[128,1,8,8,128]{4,3,2,1,0:T(8,128)(2,1)}, bf16[128,1,8,8,128]{4,3,2,1,0:T(8,128)(2,1)S(1)}, u32[]{:S(2)}) copy-start(bf16[128,1,8,8,128]{4,3,2,1,0:T(8,128)(2,1)S(1)} %get-tuple-element.8) | copy-start | bytes 6291460
  219.0 12.2 %copy-start = (f32[128,1,8,8,128]{4,3,2,1,0:T(8,128)}, f32[128,1,8,8,128]{4,3,2,1,0:T(8,128)S(1)}, u32[]{:S(2)}) copy-start(f32[128,1,8,8,128]{4,3,2,1,0:T(8,128)S(1)} %get-tuple-element.9) | copy-start | bytes 12582916
  226.5 4.7 %copy-start.1 = (bf16[8,1024,192]{1,2,0:T(8,128)(2,1)}, bf16[8,1024,192]{1,2,0:T(8,128)(2,1)S(1)}, u32[]{:S(2)}) copy-start(bf16[8,1024,192]{1,2,0:T(8,128)(2,1)S(1)} %fusion.9) | copy-start | bytes 9437188
  235.7 16.8 %copy-start.7 = (s32[64,1]{0,1:T(1,128)S(1)}, s32[64,1]{0,1:T(1,128)}, u32[]{:S(2)}) copy-start(s32[64,1]{0,1:T(1,128)} %param.10) | copy-start | bytes 772
  237.4 121.8 %all-to-all-start.1 = ((bf16[64,18,8,128]{3,2,1,0:T(8,128)(2,1)}), bf16[64,18,8,128]{3,2,1,0:T(8,128)(2,1)}, u32[]{:S(2)}, u32[]{:S(2)}) async-start(bf16[64,18,8,128]{3,2,1,0:T(8,128)(2,1)} %pad_maximum_fusion), calls=%async_computation.1 | async-start | bytes 4718592 | tf_op jit(solution)/shard_map/all_to_all | solution.py:94
where the time goes:
time: 386 us; the launch traced here: 385 us
  waiting for transfers between devices  281 us (73%)
  starting transfers between devices  37.5 us (10%)
  blocking collectives  21 us (5%)
  matrix products  15.4 us (4%)
  other arithmetic  15.1 us (4%)
  local copies, waits for them, and re-layouts  13.9 us (4%)
    all_to_all x1, waiting for transfers between devices, shards(): lax.all_to_all(send_both, 'spec', split_axis=0, concat_axis=0, tiled=True)  184 us
    all_to_all x1, waiting for transfers between devices, shards(): lax.all_to_all(going_back, 'spec', split_axis=0, concat_axis=0, tiled=True)  96.9 us
    all_to_all x1, starting transfers between devices, shards(): lax.all_to_all(send_both, 'spec', split_axis=0, concat_axis=0, tiled=True)  22.3 us
    psum x1, blocking collectives, shards(): gain_grad = lax.psum(spec_sum, 'grp')  21 us
    all_to_all x1, starting transfers between devices, shards(): lax.all_to_all(going_back, 'spec', split_axis=0, concat_axis=0, tiled=True)  15.2 us
  transfers between devices with their start and end apart: 2, of which 2 were waited for; matrix products, arithmetic and copies ran while one was open for 3% of the time, Pallas kernels for 0%

commit v1 on v0

--- a/solution.py
+++ b/solution.py
@@ -95,7 +95,7 @@
     spec_sum = jnp.sum(came_back[:, CAP * qtok_here :].astype(jnp.float32), axis=(0, 1)).reshape(
         width
     )
-    gain_grad = lax.psum(spec_sum, "grp")
+    gain_grad = jnp.sum(lax.all_gather(spec_sum, "grp"), axis=0)
     came_back = came_back[:, : CAP * qtok_here]
     home_grads = jnp.take(
         came_back.reshape(slot_count, qtok_here, HEADS, width // HEADS),

time: 386 us -> 387 us (level)
    all_gather x0 -> x1, blocking collectives: none -> 21.8 us  [shards(): gain_grad = jnp.sum(lax.all_gather(spec_sum, 'grp'), axis=0)]
    psum x1 -> x0, blocking collectives: 21 us -> none  [shards(): gain_grad = lax.psum(spec_sum, 'grp')]
where the time goes in v1:
time: 387 us; the launch traced here: 386 us
  waiting for transfers between devices  281 us (73%)
  starting transfers between devices  37.5 us (10%)
  blocking collectives  21.8 us (6%)
  other arithmetic  15.7 us (4%)
  matrix products  15.4 us (4%)
  local copies, waits for them, and re-layouts  13.9 us (4%)
    all_to_all x1, waiting for transfers between devices, shards(): lax.all_to_all(send_both, 'spec', split_axis=0, concat_axis=0, tiled=True)  184 us
    all_to_all x1, waiting for transfers between devices, shards(): lax.all_to_all(going_back, 'spec', split_axis=0, concat_axis=0, tiled=True)  96.9 us
    all_to_all x1, starting transfers between devices, shards(): lax.all_to_all(send_both, 'spec', split_axis=0, concat_axis=0, tiled=True)  22.3 us
    all_gather x1, blocking collectives, shards(): gain_grad = jnp.sum(lax.all_gather(spec_sum, 'grp'), axis=0)  21.8 us
    all_to_all x1, starting transfers between devices, shards(): lax.all_to_all(going_back, 'spec', split_axis=0, concat_axis=0, tiled=True)  15.2 us
  transfers between devices with their start and end apart: 2, of which 2 were waited for; matrix products, arithmetic and copies ran while one was open for 3% of the time, Pallas kernels for 0%

profile of v1, /device:TPU:1, one launch (start us, length us, event | category | flops | bytes accessed | tf_op | source)
XLA Modules:
  0.0 386.4 jit_solution(14655806935987668711)
XLA Ops:
  0.6 0.7 fusion.36
  1.4 0.1 reduce_window_sum.11
  1.5 0.8 select_reduce_fusion
  2.3 0.7 multiply_add_fusion
  3.0 0.6 iota_reduce_fusion
  3.6 0.1 fusion.37
  3.7 2.2 copy_bitcast_fusion.1
  5.9 0.2 fusion.10
  6.1 3.1 gather_fusion
  9.1 0.0 copy-start.3
  9.1 0.0 copy-start.4
  9.1 0.0 copy-start.6
  9.1 22.3 %all-to-all-start = ((bf16[64,32,8,128]{3,2,1,0:T(8,128)(2,1)}), bf16[64,32,8,128]{3,2,1,0:T(8,128)(2,1)}, u32[]{:S(2)}, u32[]{:S(2)}) async-start(bf16[64,32,8,128]{3,2,1,0:T(8,128)(2,1)} %bitcast.82), calls=%async_computation | async-start | bytes 8388608 | tf_op jit(solution)/shard_map/all_to_all | solution.py:81
  31.4 0.0 copy-done.3
  31.4 0.1 copy.46
  31.5 0.0 copy-done.4
  31.5 0.1 copy.47
  31.6 0.0 copy-done.6
  31.6 0.0 copy-start.5
  31.6 184.3 %all-to-all-done = bf16[64,32,8,128]{3,2,1,0:T(8,128)(2,1)} async-done(((bf16[64,32,8,128]{3,2,1,0:T(8,128)(2,1)}), bf16[64,32,8,128]{3,2,1,0:T(8,128)(2,1)}, u32[]{:S(2)}, u32[]{:S(2)}) %all-to-all-start) | async-done | bytes 4194336 | tf_op jit(solution)/shard_map/all_to_all | solution.py:81
  215.9 3.1 fusion.41
  219.0 0.0 copy-start.2
  219.0 0.0 copy-start
  219.0 1.4 fusion.25
  220.4 5.1 %fusion.42 = (f32[8,1024]{1,0:T(8,128)S(1)}, f32[8,1024,192]{1,2,0:T(8,128)S(1)}) fusion(f32[8,1024,192]{1,2,0:T(8,128)S(1)} %fusion.25), kind=kOutput, calls=%fused_computation.65 | output fusion | flops 6291647 | bytes 12615680 | tf_op jit(solution)/shard_map/sub | solution.py:27
  225.5 1.0 fusion.9
  226.5 0.0 copy-start.1
  226.5 0.0 copy-done.5
  226.5 2.3 multiply_reduce_fusion.1
  228.8 0.0 copy-done.2
  228.9 2.3 multiply_convert_fusion
  231.2 0.0 copy-done
  231.2 0.0 copy-done.1
  231.2 2.0 multiply_convert_fusion.1
  233.2 2.4 copy.40
  235.7 0.0 copy-start.7
  235.8 1.6 pad_maximum_fusion
  237.4 15.2 %all-to-all-start.1 = ((bf16[64,18,8,128]{3,2,1,0:T(8,128)(2,1)}), bf16[64,18,8,128]{3,2,1,0:T(8,128)(2,1)}, u32[]{:S(2)}, u32[]{:S(2)}) async-start(bf16[64,18,8,128]{3,2,1,0:T(8,128)(2,1)} %pad_maximum_fusion), calls=%async_computation.1 | async-start | bytes 4718592 | tf_op jit(solution)/shard_map/all_to_all | solution.py:94
  252.5 0.0 copy-done.7
  252.6 3.6 fusion.20
  256.2 0.3 copy.41
  256.5 0.9 broadcast_in_dim_reshape.6
  257.4 3.7 fusion.21
  261.1 0.3 copy.42
  261.4 0.9 broadcast_in_dim_reshape.7
  262.3 96.9 %all-to-all-done.1 = bf16[64,18,8,128]{3,2,1,0:T(8,128)(2,1)} async-done(((bf16[64,18,8,128]{3,2,1,0:T(8,128)(2,1)}), bf16[64,18,8,128]{3,2,1,0:T(8,128)(2,1)}, u32[]{:S(2)}, u32[]{:S(2)}) %all-to-all-start.1) | async-done | bytes 2359328 | tf_op jit(solution)/shard_map/all_to_all | solution.py:94
  359.2 1.7 slice.22
  360.9 0.7 gather_fusion.1
  361.7 1.2 copy.87
  362.9 1.1 convert_reduce_fusion
  364.0 21.8 %all-gather = f32[8,1,1024]{2,1,0:T(1,128)S(1)} all-gather(f32[1,1,1024]{2,1,0:T(1,128)S(1)} %bitcast.96), channel_id=1, replica_groups=mesh['grp'=8,'spec'=64] {'grp'}, dimensions={0}, use_global_device_ids=true | all-gather | bytes 36864 | tf_op jit(solution)/shard_map/all_gather | solution.py:98
  385.8 0.6 reduce_sum.65
  (8 shorter events, 0.1 us)
Async XLA Ops:
  9.1 22.3 %copy-start.3 = (bf16[1,192,1024]{2,1,0:T(8,128)(2,1)S(1)}, bf16[1,192,1024]{2,1,0:T(8,128)(2,1)}, u32[]{:S(2)}) copy-start(bf16[1,192,1024]{2,1,0:T(8,128)(2,1)} %param.8) | copy-start | bytes 1179652
  9.1 22.4 %copy-start.4 = (bf16[1,192,1024]{2,1,0:T(8,128)(2,1)S(1)}, bf16[1,192,1024]{2,1,0:T(8,128)(2,1)}, u32[]{:S(2)}) copy-start(bf16[1,192,1024]{2,1,0:T(8,128)(2,1)} %param.9) | copy-start | bytes 1179652
  9.1 22.5 %copy-start.6 = (f32[1024]{0:T(1024)S(1)}, f32[1024]{0:T(1024)}, u32[]{:S(2)}) copy-start(f32[1024]{0:T(1024)} %param.11) | copy-start | bytes 12292
  9.1 206.8 %all-to-all-start = ((bf16[64,32,8,128]{3,2,1,0:T(8,128)(2,1)}), bf16[64,32,8,128]{3,2,1,0:T(8,128)(2,1)}, u32[]{:S(2)}, u32[]{:S(2)}) async-start(bf16[64,32,8,128]{3,2,1,0:T(8,128)(2,1)} %bitcast.82), calls=%async_computation | async-start | bytes 8388608 | tf_op jit(solution)/shard_map/all_to_all | solution.py:81
  31.6 194.9 %copy-start.5 = (bf16[24,8,8,128]{3,2,1,0:T(8,128)(2,1)}, bf16[24,8,8,128]{3,2,1,0:T(8,128)(2,1)S(1)}, u32[]{:S(2)}) copy-start(bf16[24,8,8,128]{3,2,1,0:T(8,128)(2,1)S(1)} %copy.47) | copy-start | bytes 1179652
  219.0 9.9 %copy-start.2 = (bf16[128,1,8,8,128]{4,3,2,1,0:T(8,128)(2,1)}, bf16[128,1,8,8,128]{4,3,2,1,0:T(8,128)(2,1)S(1)}, u32[]{:S(2)}) copy-start(bf16[128,1,8,8,128]{4,3,2,1,0:T(8,128)(2,1)S(1)} %get-tuple-element.8) | copy-start | bytes 6291460
  219.0 12.2 %copy-start = (f32[128,1,8,8,128]{4,3,2,1,0:T(8,128)}, f32[128,1,8,8,128]{4,3,2,1,0:T(8,128)S(1)}, u32[]{:S(2)}) copy-start(f32[128,1,8,8,128]{4,3,2,1,0:T(8,128)S(1)} %get-tuple-element.9) | copy-start | bytes 12582916
  226.5 4.7 %copy-start.1 = (bf16[8,1024,192]{1,2,0:T(8,128)(2,1)}, bf16[8,1024,192]{1,2,0:T(8,128)(2,1)S(1)}, u32[]{:S(2)}) copy-start(bf16[8,1024,192]{1,2,0:T(8,128)(2,1)S(1)} %fusion.9) | copy-start | bytes 9437188
  235.7 16.8 %copy-start.7 = (s32[64,1]{0,1:T(1,128)S(1)}, s32[64,1]{0,1:T(1,128)}, u32[]{:S(2)}) copy-start(s32[64,1]{0,1:T(1,128)} %param.10) | copy-start | bytes 772
  237.4 121.8 %all-to-all-start.1 = ((bf16[64,18,8,128]{3,2,1,0:T(8,128)(2,1)}), bf16[64,18,8,128]{3,2,1,0:T(8,128)(2,1)}, u32[]{:S(2)}, u32[]{:S(2)}) async-start(bf16[64,18,8,128]{3,2,1,0:T(8,128)(2,1)} %pad_maximum_fusion), calls=%async_computation.1 | async-start | bytes 4718592 | tf_op jit(solution)/shard_map/all_to_all | solution.py:94
